TPU v7x, 256 devices: a whole 4x4x8 slice. The times are simulated.
256 devices in a mesh: seq: 64 (over x, z, core), ch: 4 (over y).
Axes of the slice: x: 4, y: 4, z: 8, core: 2. Of those that a mesh axis runs over, the one named last changes fastest.
Arguments:
- inputs: bfloat16 [8192, 4096], P('seq'), may hold values from -6 to 6
- norm_gain: float32 [4096], replicated, may hold values from 0.1 to 1.9
- in_weight: bfloat16 [4096, 3, 1024], P('seq', None, 'ch'), may hold values from -0.09375 to 0.09375
- short_filter: float32 [3, 3, 1024], P(None, None, 'ch'), may hold values from -4 to 4
- long_filter: float32 [8192, 1024], P('seq', 'ch'), may hold values from -2.2 to 2.2
- conv_bias: float32 [1024], P('ch'), may hold values from -4 to 4
- out_weight: bfloat16 [1024, 4096], P('ch', 'seq'), may hold values from -0.1875 to 0.1875
- out_grad: bfloat16 [8192, 4096], P('seq'), may hold values from -6 to 6
Outputs:
- block_out: bfloat16 [8192, 4096], P('seq', 'ch')
- in_grad: bfloat16 [8192, 4096], P('seq')
- filter_grad: float32 [8192, 1024], P('seq', 'ch')
All inputs are finite; a program needn't handle non-finite values.
Results may differ from a plain program's by a relative error of at most 0.013.
Values may be sent and summed in bfloat16 or wider, within the bound.
No kernel may reach another device: no remote copies, remote signals or barrier semaphores. Data moves between devices by JAX's collectives and lax.ppermute only.
A program may use at most 64 MiB of HBM per device.

v0:
```python
import math
import jax
import jax.numpy as jnp
from jax import lax
from jax.sharding import PartitionSpec as P

epsilon = 1e-05
highest = lax.Precision.HIGHEST


def passed_along(block, axis, distance):
    devices = range(lax.axis_size(axis))
    route = [(i - distance, i) for i in devices if i - distance in devices]
    return lax.ppermute(block, axis, route)


def doubled_gather(block, axis):
    devices = lax.axis_size(axis)
    place = lax.axis_index(axis)
    bits = devices.bit_length() - 1
    assert 1 << bits == devices
    gathered = block
    for bit in reversed(range(bits)):
        route = [(i, i ^ 1 << bit) for i in range(devices)]
        arrived = lax.ppermute(gathered, axis, route)
        lower = place >> bit & 1 == 0
        gathered = jnp.where(lower, jnp.stack([gathered, arrived]), jnp.stack([arrived, gathered]))
    gathered = gathered.transpose(tuple(reversed(range(bits))) + tuple(range(bits, gathered.ndim)))
    return gathered.reshape((devices * block.shape[0],) + block.shape[1:])


def halved_sum(partial, axis):
    devices = lax.axis_size(axis)
    place = lax.axis_index(axis)
    bits = devices.bit_length() - 1
    assert 1 << bits == devices
    rows, width = partial.shape
    share = width // devices
    held = partial.reshape((rows,) + (2,) * bits + (share,))
    held = held.transpose((0,) + tuple(range(bits, 0, -1)) + (bits + 1,)).astype(jnp.float32)
    for bit in range(bits):
        route = [(i, i ^ 1 << bit) for i in range(devices)]
        mine = place >> bit & 1
        kept = lax.dynamic_index_in_dim(held, mine, 1, keepdims=False)
        given = lax.dynamic_index_in_dim(held, 1 - mine, 1, keepdims=False)
        arrived = lax.ppermute(given.astype(jnp.bfloat16), axis, route)
        held = kept + arrived.astype(jnp.float32)
    return held


def to_columns(signals):
    return lax.all_to_all(signals, "seq", split_axis=1, concat_axis=2, tiled=True)


def to_rows(signals):
    count, chans, seq_total = signals.shape
    devices = lax.axis_size("seq")
    local_rows = seq_total // devices
    pieces = signals.reshape(count, chans, devices, local_rows).transpose(2, 0, 1, 3)
    arrived = lax.all_to_all(pieces, "seq", split_axis=0, concat_axis=0, tiled=True)
    return arrived.transpose(1, 3, 0, 2).reshape(count, local_rows, devices * chans)


def turn_table(rows, cols, period, sign):
    turns = jnp.arange(rows, dtype=jnp.int32)[:, None] * jnp.arange(cols, dtype=jnp.int32)[None, :]
    turns = lax.optimization_barrier(turns)
    phases = sign * 2.0 * math.pi / period * (turns % period).astype(jnp.float32)
    return (jnp.cos(phases), jnp.sin(phases))


def fft_sizes(seq_total):
    total = 2 * seq_total
    inner = 1
    while inner * inner < total:
        inner *= 2
    return (total // inner, inner)


def forward_dft(signals):
    count, chans, seq_total = signals.shape
    outer, inner = fft_sizes(seq_total)
    grid = signals.reshape(count, chans, outer // 2, inner)
    cos_out, sin_out = turn_table(outer, outer // 2, outer, 1.0)
    first = jnp.einsum(
        "kn,ucnm->uckm", jnp.concatenate([cos_out, -sin_out], 0), grid, precision=lax.Precision.HIGH
    )
    first_real, first_imag = (first[:, :, :outer], first[:, :, outer:])
    cos_tw, sin_tw = turn_table(outer, inner, outer * inner, 1.0)
    turned_real = first_real * cos_tw + first_imag * sin_tw
    turned_imag = first_imag * cos_tw - first_real * sin_tw
    cos_in, sin_in = turn_table(inner, inner, inner, 1.0)
    rotation = jnp.concatenate(
        [jnp.concatenate([cos_in, -sin_in], 1), jnp.concatenate([sin_in, cos_in], 1)], 0
    )
    joined = jnp.concatenate([turned_real, turned_imag], -1)
    spec = jnp.einsum("uckm,mj->uckj", joined, rotation, precision=lax.Precision.HIGH)
    return (spec[..., :inner], spec[..., inner:])


def inverse_dft(spec_real, spec_imag):
    count, chans, outer, inner = spec_real.shape
    cos_in, sin_in = turn_table(inner, inner, inner, 1.0)
    rotation = jnp.concatenate(
        [jnp.concatenate([cos_in, sin_in], 1), jnp.concatenate([-sin_in, cos_in], 1)], 0
    )
    joined = jnp.concatenate([spec_real, spec_imag], -1)
    back = jnp.einsum("uckj,jm->uckm", joined, rotation, precision=lax.Precision.HIGH)
    back_real, back_imag = (back[..., :inner], back[..., inner:])
    cos_tw, sin_tw = turn_table(outer, inner, outer * inner, 1.0)
    turned_real = back_real * cos_tw - back_imag * sin_tw
    turned_imag = back_imag * cos_tw + back_real * sin_tw
    cos_out, sin_out = turn_table(outer, outer // 2, outer, 1.0)
    grid = jnp.einsum(
        "kn,uckm->ucnm",
        jnp.concatenate([cos_out, -sin_out], 0),
        jnp.concatenate([turned_real, turned_imag], 2),
        precision=lax.Precision.HIGH,
    )
    return grid.reshape(count, chans, outer * inner // 2) / float(outer * inner)


def per_device(
    inputs, norm_gain, in_weight, short_filter, long_filter, conv_bias, out_weight, out_grad
):
    local_rows = inputs.shape[0]
    model_width = inputs.shape[1]
    slab_width = long_filter.shape[1]
    taps = short_filter.shape[1]
    wide_inputs = inputs.astype(jnp.float32)
    inv_rms = lax.rsqrt(jnp.mean(wide_inputs * wide_inputs, axis=1, keepdims=True) + epsilon)
    normed = (wide_inputs * inv_rms * norm_gain).astype(jnp.bfloat16)
    in_panel, out_panel = (
        lax.all_gather(in_weight.reshape(in_weight.shape[0], -1), "seq", axis=0, tiled=True),
        doubled_gather(out_weight.T, "seq").T,
    )
    in_flat = in_panel.reshape(model_width, 3 * slab_width)
    projected = jnp.dot(normed, in_flat, preferred_element_type=jnp.float32)
    projected = projected.astype(jnp.bfloat16).reshape(local_rows, 3, slab_width)
    upper_rim = passed_along(projected[local_rows - (taps - 1) :], "seq", 1)
    extended = jnp.concatenate([upper_rim, projected], 0).astype(jnp.float32)
    mixed = jnp.zeros((local_rows, 3, slab_width), jnp.float32)
    for offset in range(taps):
        begin = taps - 1 - offset
        mixed = mixed + short_filter[:, offset, :][None] * extended[begin : begin + local_rows]
    query_br = mixed[:, 0]
    key_br = mixed[:, 1]
    value_br = mixed[:, 2]
    product = key_br * value_br
    gate_grad = jnp.dot(out_grad, out_panel.T, preferred_element_type=jnp.float32)
    carried = gate_grad * query_br
    filt_real, filt_imag = forward_dft(to_columns(long_filter.T[None]))
    filt_real, filt_imag = (filt_real[0], filt_imag[0])
    columns = to_columns(jnp.stack([product, carried]).transpose(0, 2, 1))
    all_real, all_imag = forward_dft(columns)
    sig_real, grad_real = (all_real[0], all_real[1])
    sig_imag, grad_imag = (all_imag[0], all_imag[1])
    conv_real = sig_real * filt_real - sig_imag * filt_imag
    conv_imag = sig_real * filt_imag + sig_imag * filt_real
    back_real = grad_real * filt_real + grad_imag * filt_imag
    back_imag = grad_imag * filt_real - grad_real * filt_imag
    pair_real = grad_real * sig_real + grad_imag * sig_imag
    pair_imag = grad_imag * sig_real - grad_real * sig_imag
    outs = inverse_dft(
        jnp.stack([conv_real, back_real, pair_real]), jnp.stack([conv_imag, back_imag, pair_imag])
    )
    returned = to_rows(outs)
    conv_out = returned[0]
    back_conv = returned[1]
    filter_grad = returned[2] * float(local_rows * lax.axis_size("seq")) ** (-0.5)
    biased = conv_out + conv_bias * product
    gated = (query_br * biased).astype(jnp.bfloat16)
    partial_out = jnp.dot(gated, out_panel, preferred_element_type=jnp.float32)
    source_grad = back_conv + conv_bias * carried
    mixed_grad = jnp.stack([gate_grad * biased, source_grad * value_br, source_grad * key_br], 1)
    lower_rim = passed_along(mixed_grad[: taps - 1], "seq", -1)
    extended_back = jnp.concatenate([mixed_grad, lower_rim], 0)
    proj_grad = jnp.zeros((local_rows, 3, slab_width), jnp.float32)
    for offset in range(taps):
        proj_grad = (
            proj_grad
            + short_filter[:, offset, :][None] * extended_back[offset : offset + local_rows]
        )
    proj_grad = proj_grad.astype(jnp.bfloat16).reshape(local_rows, 3 * slab_width)
    partial_grad = jnp.dot(proj_grad, in_flat.T, preferred_element_type=jnp.float32)
    ch_size = lax.axis_size("ch")
    feature_share = model_width // ch_size
    partial_inner = jnp.sum(partial_grad * (norm_gain * wide_inputs), axis=1, keepdims=True)
    inner_high = partial_inner.astype(jnp.bfloat16)
    inner_low = (partial_inner - inner_high.astype(jnp.float32)).astype(jnp.bfloat16)
    extra = jnp.concatenate(
        [inner_high, inner_low, jnp.zeros((local_rows, 126), jnp.bfloat16)], axis=1
    )
    payload = jnp.concatenate(
        [
            partial_out.astype(jnp.bfloat16)
            .reshape(local_rows, ch_size, feature_share)
            .transpose(1, 0, 2),
            partial_grad.astype(jnp.bfloat16)
            .reshape(local_rows, ch_size, feature_share)
            .transpose(1, 0, 2),
            jnp.broadcast_to(extra[None], (ch_size, local_rows, 128)),
        ],
        axis=2,
    )
    reduced = lax.psum_scatter(payload, "ch", scatter_dimension=0).astype(jnp.float32)
    summed = reduced[:, :feature_share]
    norm_grad = reduced[:, feature_share : 2 * feature_share]
    inner_at = 2 * feature_share
    inner_term = (
        reduced[:, inner_at : inner_at + 1] + reduced[:, inner_at + 1 : inner_at + 2]
    ) / model_width
    feature_begin = lax.axis_index("ch") * feature_share
    residual = lax.dynamic_slice_in_dim(wide_inputs, feature_begin, feature_share, 1)
    block_out = (residual + summed).astype(jnp.bfloat16)
    gain_share = lax.dynamic_slice_in_dim(norm_gain, feature_begin, feature_share, 0)
    inputs_share = lax.dynamic_slice_in_dim(wide_inputs, feature_begin, feature_share, 1)
    grad_share = lax.dynamic_slice_in_dim(out_grad, feature_begin, feature_share, 1)
    weighted = norm_grad * gain_share
    in_grad_share = (
        grad_share.astype(jnp.float32) + weighted * inv_rms - inputs_share * inv_rms**3 * inner_term
    ).astype(jnp.bfloat16)
    in_grad = (
        doubled_gather(in_grad_share[None], "ch")
        .transpose(1, 0, 2)
        .reshape(local_rows, model_width)
    )
    return (block_out, in_grad, filter_grad)


def solution(mesh):
    return jax.shard_map(
        per_device,
        mesh=mesh,
        in_specs=(
            P("seq", None),
            P(),
            P("seq", None, "ch"),
            P(None, None, "ch"),
            P("seq", "ch"),
            P("ch"),
            P("ch", "seq"),
            P("seq", None),
        ),
        out_specs=(P("seq", "ch"), P("seq", None), P("seq", "ch")),
        check_vma=False,
    )
```

profile of v0, /device:TPU:2, one launch (start us, length us, event | category | flops | bytes accessed | tf_op | source)
XLA Modules:
  0.0 249.4 jit_solution(18105231908628929155)
XLA Ops:
  7.2 1.5 copy.156
  8.8 2.2 collective-permute-start.1
  11.0 1.7 copy.126
  12.6 11.2 %all-to-all-start.1 = ((f32[1,256,128]{2,0,1:T(1,128)}), f32[1,256,128]{2,0,1:T(1,128)}, u32[]{:S(2)}, u32[]{:S(2)}) async-start(f32[1,256,128]{2,0,1:T(1,128)} %bitcast.1), calls=%async_computation.1 | async-start | bytes 262144 | tf_op jit(solution)/shard_map/all_to_all | solution.py:52
  28.5 2.5 %collective-permute-done.2 = bf16[2,64,256]{2,1,0:T(8,128)(2,1)S(1)} collective-permute-done((bf16[2,64,256]{2,1,0:T(8,128)(2,1)S(1)}, bf16[2,64,256]{2,1,0:T(8,128)(2,1)S(1)}, u32[]{:S(2)}, u32[]{:S(2)}) %collective-permute-start.2) | collective-permute-done | bytes 65568 | tf_op jit(solution)/shard_map/ppermute | solution.py:25
  31.0 5.2 %collective-permute-start.3 = (bf16[2,2,64,256]{3,2,0,1:T(8,128)(2,1)S(1)}, bf16[2,2,64,256]{3,2,0,1:T(8,128)(2,1)S(1)}, u32[]{:S(2)}, u32[]{:S(2)}) collective-permute-start(bf16[2,2,64,256]{3,2,0,1:T(8,128)(2,1)S(1)} %maximum_select_fusion.7), channel_id=1, source_target_pairs={{0,32},{4,36},{8,40},{12,44},{16,48},{20,52},{24,56},{28,60},{32,0... | collective-permute-start | bytes 393224 | tf_op jit(solution)/shard_map/ppermute | solution.py:25
  36.3 6.4 %collective-permute-done.3 = bf16[2,2,64,256]{3,2,0,1:T(8,128)(2,1)S(1)} collective-permute-done((bf16[2,2,64,256]{3,2,0,1:T(8,128)(2,1)S(1)}, bf16[2,2,64,256]{3,2,0,1:T(8,128)(2,1)S(1)}, u32[]{:S(2)}, u32[]{:S(2)}) %collective-permute-start.3) | collective-permute-done | bytes 131104 | tf_op jit(solution)/shard_map/ppermute | solution.py:25
  42.7 3.4 %collective-permute-start.4 = (bf16[2,2,2,64,256]{4,3,0,1,2:T(8,128)(2,1)S(1)}, bf16[2,2,2,64,256]{4,3,0,1,2:T(8,128)(2,1)S(1)}, u32[]{:S(2)}, u32[]{:S(2)}) collective-permute-start(bf16[2,2,2,64,256]{4,3,0,1,2:T(8,128)(2,1)S(1)} %maximum_select_fusion.6), channel_id=1, source_target_pairs={{0,16},{4,20},{8,24},{12,28},{16,0},{20,4},{24,8},{28,12},{32,48},... | collective-permute-start | bytes 786440 | tf_op jit(solution)/shard_map/ppermute | solution.py:25
  46.3 11.2 %collective-permute-done.4 = bf16[2,2,2,64,256]{4,3,0,1,2:T(8,128)(2,1)S(1)} collective-permute-done((bf16[2,2,2,64,256]{4,3,0,1,2:T(8,128)(2,1)S(1)}, bf16[2,2,2,64,256]{4,3,0,1,2:T(8,128)(2,1)S(1)}, u32[]{:S(2)}, u32[]{:S(2)}) %collective-permute-start.4) | collective-permute-done | bytes 262176 | tf_op jit(solution)/shard_map/ppermute | solution.py:25
  60.3 11.2 %collective-permute-done.5 = bf16[2,2,2,2,64,256]{5,4,0,1,2,3:T(8,128)(2,1)S(1)} collective-permute-done((bf16[2,2,2,2,64,256]{5,4,0,1,2,3:T(8,128)(2,1)S(1)}, bf16[2,2,2,2,64,256]{5,4,0,1,2,3:T(8,128)(2,1)S(1)}, u32[]{:S(2)}, u32[]{:S(2)}) %collective-permute-start.5) | collective-permute-done | bytes 524320 | tf_op jit(solution)/shard_map/ppermute | solution.py:25
  74.6 25.0 %all-gather.2.cloned.1.call-done = bf16[4096,768]{1,0:T(8,128)(2,1)} async-done(((bf16[64,768]{1,0:T(8,128)(2,1)}), bf16[4096,768]{1,0:T(8,128)(2,1)}) %all-gather.2.cloned.1.call-update) | async-done | bytes 6291472 | tf_op jit(solution)/shard_map/all_gather | solution.py:133
  99.6 3.9 %convolution_convert_fusion.1 = bf16[128,768]{1,0:T(8,128)(2,1)S(1)} fusion(bf16[4096,768]{1,0:T(8,128)(2,1)} %all-gather.2.cloned.1.call-done, bf16[128,4096]{1,0:T(8,128)(2,1)S(1)} %copy-done, f32[4096]{0:T(1024)S(1)} %copy-done.17, f32[128]{0:T(128)S(1)} %get-tuple-element.53), kind=kOutput, calls=%fused_computation.26 | convolution fusion | flops 807501824 | bytes 7553536 | tf_op jit(solution)/shard_map/dot_general | solution.py:137
  104.1 2.1 collective-permute-start
  107.8 3.6 %collective-permute-done = bf16[2,3,256]{2,0,1:T(2,128)(2,1)S(1)} collective-permute-done((bf16[2,3,256]{2,0,1:T(2,128)(2,1)}, bf16[2,3,256]{2,0,1:T(2,128)(2,1)S(1)}, u32[]{:S(2)}, u32[]{:S(2)}) %collective-permute-start) | collective-permute-done | bytes 3104 | tf_op jit(solution)/shard_map/ppermute | solution.py:14
  112.3 1.8 copy.120
  114.1 6.5 %all-to-all-start = ((f32[2,256,128]{2,0,1:T(2,128)}), f32[2,256,128]{2,0,1:T(2,128)}, u32[]{:S(2)}, u32[]{:S(2)}) async-start(f32[2,256,128]{2,0,1:T(2,128)} %copy.120), calls=%async_computation | async-start | bytes 524288 | tf_op jit(solution)/shard_map/all_to_all | solution.py:52
  124.4 2.3 convolution_bitcast_fusion.1
  126.8 5.3 %all-to-all-done = f32[2,256,128]{2,0,1:T(2,128)} async-done(((f32[2,256,128]{2,0,1:T(2,128)}), f32[2,256,128]{2,0,1:T(2,128)}, u32[]{:S(2)}, u32[]{:S(2)}) %all-to-all-start) | async-done | bytes 262176 | tf_op jit(solution)/shard_map/all_to_all | solution.py:52
  132.1 1.6 convolution_bitcast_fusion
  139.3 6.6 %all-to-all-start.2 = ((f32[64,3,4,128]{3,2,1,0:T(4,128)}), f32[64,3,4,128]{3,2,1,0:T(4,128)}, u32[]{:S(2)}, u32[]{:S(2)}) async-start(f32[64,3,4,128]{3,2,1,0:T(4,128)} %copy.131), calls=%async_computation.2 | async-start | bytes 786432 | tf_op jit(solution)/shard_map/all_to_all | solution.py:60
  146.6 13.4 %all-to-all-done.2 = f32[64,3,4,128]{3,2,1,0:T(4,128)} async-done(((f32[64,3,4,128]{3,2,1,0:T(4,128)}), f32[64,3,4,128]{3,2,1,0:T(4,128)}, u32[]{:S(2)}, u32[]{:S(2)}) %all-to-all-start.2) | async-done | bytes 393248 | tf_op jit(solution)/shard_map/all_to_all | solution.py:60
  160.0 1.8 slice_multiply_fusion.6
  161.7 1.7 copy.132
  163.4 1.7 copy.134
  165.1 1.7 copy.135
  167.9 2.9 %collective-permute-start.7 = (f32[2,3,256]{2,0,1:T(2,128)S(1)}, f32[2,3,256]{2,0,1:T(2,128)S(1)}, u32[]{:S(2)}, u32[]{:S(2)}) collective-permute-start(f32[2,3,256]{2,0,1:T(2,128)S(1)} %slice.165), channel_id=1, source_target_pairs={{4,0},{8,4},{12,8},{16,12},{20,16},{24,20},{28,24},{32,28},{36,32}... | collective-permute-start | bytes 18440 | tf_op jit(solution)/shard_map/ppermute | solution.py:14
  172.5 5.0 %fusion.90 = (bf16[128,4096]{1,0:T(8,128)(2,1)S(1)}, f32[128]{0:T(128)S(1)}) fusion(bf16[128,4096]{1,0:T(8,128)(2,1)S(1)} %copy-done, f32[4096]{0:T(1024)S(1)} %copy-done.18, bf16[128,768]{0,1:T(8,128)(2,1)S(1)} %bitcast.206, bf16[4096,768]{1,0:T(8,128)(2,1)} %all-gather.2.cloned.1.call-done), kind=kOutput, calls=%fused_computation.176 | convolution fusion | flops 807927680 | bytes 8602112 | tf_op jit(solution)/shard_map/dot_general | solution.py:184
  180.7 1.6 pad_maximum_fusion
  182.6 32.0 %reduce-scatter.2.cloned.1.call-done = bf16[1,128,2176]{2,1,0:T(8,128)(2,1)} async-done(((bf16[4,128,2176]{2,1,0:T(8,128)(2,1)}), bf16[1,128,2176]{2,1,0:T(8,128)(2,1)}) %reduce-scatter.2.cloned.1.call-update) | async-done | bytes 557072 | tf_op jit(solution)/shard_map/reduce_scatter | solution.py:205
  216.0 1.9 fusion.29
  219.3 8.0 %collective-permute-done.8 = bf16[1,128,1024]{2,1,0:T(8,128)(2,1)S(1)} collective-permute-done((bf16[1,128,1024]{2,1,0:T(8,128)(2,1)S(1)}, bf16[1,128,1024]{2,1,0:T(8,128)(2,1)S(1)}, u32[]{:S(2)}, u32[]{:S(2)}) %collective-permute-start.8) | collective-permute-done | bytes 262176 | tf_op jit(solution)/shard_map/ppermute | solution.py:25
  228.6 11.7 %collective-permute-done.9 = bf16[2,1,128,1024]{3,2,1,0:T(8,128)(2,1)S(1)} collective-permute-done((bf16[2,1,128,1024]{3,2,1,0:T(8,128)(2,1)S(1)}, bf16[2,1,128,1024]{3,2,1,0:T(8,128)(2,1)S(1)}, u32[]{:S(2)}, u32[]{:S(2)}) %collective-permute-start.9) | collective-permute-done | bytes 524320 | tf_op jit(solution)/shard_map/ppermute | solution.py:25
  (137 shorter events, 36.0 us)
Async XLA Ops:
  7.2 92.5 %all-gather.2.cloned.1.call-start = ((), (), s32[]{:S(2)}) async-start(), calls=%async_computation.4 | async-start | bytes 6389760 | tf_op jit(solution)/shard_map/all_gather | solution.py:133
  8.8 16.6 %collective-permute-start.1 = (bf16[64,256]{1,0:T(8,128)(2,1)}, bf16[64,256]{1,0:T(8,128)(2,1)S(1)}, u32[]{:S(2)}, u32[]{:S(2)}) collective-permute-start(bf16[64,256]{1,0:T(8,128)(2,1)} %bitcast.213), channel_id=1, source_target_pairs={{0,128},{4,132},{8,136},{12,140},{16,144},{20,148},{24,152},{28,15... | collective-permute-start | bytes 98312 | tf_op jit(solution)/shard_map/ppermute | solution.py:25
  12.6 101.5 %all-to-all-start.1 = ((f32[1,256,128]{2,0,1:T(1,128)}), f32[1,256,128]{2,0,1:T(1,128)}, u32[]{:S(2)}, u32[]{:S(2)}) async-start(f32[1,256,128]{2,0,1:T(1,128)} %bitcast.1), calls=%async_computation.1 | async-start | bytes 262144 | tf_op jit(solution)/shard_map/all_to_all | solution.py:52
  26.2 4.8 %collective-permute-start.2 = (bf16[2,64,256]{2,1,0:T(8,128)(2,1)S(1)}, bf16[2,64,256]{2,1,0:T(8,128)(2,1)S(1)}, u32[]{:S(2)}, u32[]{:S(2)}) collective-permute-start(bf16[2,64,256]{2,1,0:T(8,128)(2,1)S(1)} %maximum_select_fusion.8), channel_id=1, source_target_pairs={{0,64},{4,68},{8,72},{12,76},{16,80},{20,84},{24,88},{28,92},{32,9... | collective-permute-start | bytes 196616 | tf_op jit(solution)/shard_map/ppermute | solution.py:25
  31.0 11.7 %collective-permute-start.3 = (bf16[2,2,64,256]{3,2,0,1:T(8,128)(2,1)S(1)}, bf16[2,2,64,256]{3,2,0,1:T(8,128)(2,1)S(1)}, u32[]{:S(2)}, u32[]{:S(2)}) collective-permute-start(bf16[2,2,64,256]{3,2,0,1:T(8,128)(2,1)S(1)} %maximum_select_fusion.7), channel_id=1, source_target_pairs={{0,32},{4,36},{8,40},{12,44},{16,48},{20,52},{24,56},{28,60},{32,0... | collective-permute-start | bytes 393224 | tf_op jit(solution)/shard_map/ppermute | solution.py:25
  42.7 14.7 %collective-permute-start.4 = (bf16[2,2,2,64,256]{4,3,0,1,2:T(8,128)(2,1)S(1)}, bf16[2,2,2,64,256]{4,3,0,1,2:T(8,128)(2,1)S(1)}, u32[]{:S(2)}, u32[]{:S(2)}) collective-permute-start(bf16[2,2,2,64,256]{4,3,0,1,2:T(8,128)(2,1)S(1)} %maximum_select_fusion.6), channel_id=1, source_target_pairs={{0,16},{4,20},{8,24},{12,28},{16,0},{20,4},{24,8},{28,12},{32,48},... | collective-permute-start | bytes 786440 | tf_op jit(solution)/shard_map/ppermute | solution.py:25
  57.5 14.0 %collective-permute-start.5 = (bf16[2,2,2,2,64,256]{5,4,0,1,2,3:T(8,128)(2,1)S(1)}, bf16[2,2,2,2,64,256]{5,4,0,1,2,3:T(8,128)(2,1)S(1)}, u32[]{:S(2)}, u32[]{:S(2)}) collective-permute-start(bf16[2,2,2,2,64,256]{5,4,0,1,2,3:T(8,128)(2,1)S(1)} %maximum_select_fusion.3), channel_id=1, source_target_pairs={{0,8},{4,12},{8,0},{12,4},{16,24},{20,28},{24,16},{28,20},{32,40},... | collective-permute-start | bytes 1572872 | tf_op jit(solution)/shard_map/ppermute | solution.py:25
  58.7 1.4 copy-start.7
  58.7 1.4 copy-start.9
  60.3 11.5 %copy-start = (bf16[128,4096]{1,0:T(8,128)(2,1)S(1)}, bf16[128,4096]{1,0:T(8,128)(2,1)}, u32[]{:S(2)}) copy-start(bf16[128,4096]{1,0:T(8,128)(2,1)} %param.8) | copy-start | bytes 3145732
  71.7 2.8 %collective-permute-start.6 = (bf16[2,2,2,2,2,64,256]{6,5,0,1,2,3,4:T(8,128)(2,1)S(1)}, bf16[2,2,2,2,2,64,256]{6,5,0,1,2,3,4:T(8,128)(2,1)S(1)}, u32[]{:S(2)}, u32[]{:S(2)}) collective-permute-start(bf16[2,2,2,2,2,64,256]{6,5,0,1,2,3,4:T(8,128)(2,1)S(1)} %maximum_select_fusion.1), channel_id=1, source_target_pairs={{0,4},{4,0},{8,12},{12,8},{16,20},{20,16},{24,28},{28,24},{32,36},... | collective-permute-start | bytes 3145736 | tf_op jit(solution)/shard_map/ppermute | solution.py:25
  72.6 27.0 %copy-start.22 = (f32[128]{0:T(128)}, f32[128]{0:T(128)S(1)}, u32[]{:S(2)}) copy-start(f32[128]{0:T(128)S(1)} %get-tuple-element.53) | copy-start | bytes 1540
  74.4 25.2 %copy-start.17 = (f32[4096]{0:T(1024)S(1)}, f32[4096]{0:T(1024)}, u32[]{:S(2)}) copy-start(f32[4096]{0:T(1024)} %param.9) | copy-start | bytes 49156
  99.6 6.6 %copy-start.2 = (bf16[128,4096]{1,0:T(8,128)(2,1)S(1)}, bf16[128,4096]{1,0:T(8,128)(2,1)}, u32[]{:S(2)}) copy-start(bf16[128,4096]{1,0:T(8,128)(2,1)} %param.15) | copy-start | bytes 3145732
  104.1 7.2 %collective-permute-start = (bf16[2,3,256]{2,0,1:T(2,128)(2,1)}, bf16[2,3,256]{2,0,1:T(2,128)(2,1)S(1)}, u32[]{:S(2)}, u32[]{:S(2)}) collective-permute-start(bf16[2,3,256]{2,0,1:T(2,128)(2,1)} %bitcast.6), channel_id=1, source_target_pairs={{0,4},{4,8},{8,12},{12,16},{16,20},{20,24},{24,28},{28,32},{32,36}... | collective-permute-start | bytes 9224 | tf_op jit(solution)/shard_map/ppermute | solution.py:14
  107.7 3.8 %copy-start.3 = (f32[128,256]{1,0:T(8,128)S(1)}, f32[128,256]{1,0:T(8,128)}, u32[]{:S(2)}) copy-start(f32[128,256]{1,0:T(8,128)} %convolution_bitcast_fusion.3) | copy-start | bytes 393220
  114.1 17.9 %all-to-all-start = ((f32[2,256,128]{2,0,1:T(2,128)}), f32[2,256,128]{2,0,1:T(2,128)}, u32[]{:S(2)}, u32[]{:S(2)}) async-start(f32[2,256,128]{2,0,1:T(2,128)} %copy.120), calls=%async_computation | async-start | bytes 524288 | tf_op jit(solution)/shard_map/all_to_all | solution.py:52
  132.1 2.7 %copy-start.4 = (f32[128,128]{1,0:T(8,128)S(1)}, f32[128,128]{1,0:T(8,128)}, u32[]{:S(2)}) copy-start(f32[128,128]{1,0:T(8,128)} %get-tuple-element.42) | copy-start | bytes 196612
  132.1 2.7 %copy-start.5 = (f32[128,128]{1,0:T(8,128)S(1)}, f32[128,128]{1,0:T(8,128)}, u32[]{:S(2)}) copy-start(f32[128,128]{1,0:T(8,128)} %get-tuple-element.44) | copy-start | bytes 196612
  132.1 2.7 %copy-start.6 = (f32[128,128]{1,0:T(8,128)S(1)}, f32[128,128]{1,0:T(8,128)}, u32[]{:S(2)}) copy-start(f32[128,128]{1,0:T(8,128)} %get-tuple-element.46) | copy-start | bytes 196612
  134.7 1.1 copy-start.1
  137.6 29.1 %copy-start.19 = (f32[256]{0:T(256)S(1)}, f32[256]{0:T(256)}, u32[]{:S(2)}) copy-start(f32[256]{0:T(256)} %param.13) | copy-start | bytes 3076
  139.3 20.7 %all-to-all-start.2 = ((f32[64,3,4,128]{3,2,1,0:T(4,128)}), f32[64,3,4,128]{3,2,1,0:T(4,128)}, u32[]{:S(2)}, u32[]{:S(2)}) async-start(f32[64,3,4,128]{3,2,1,0:T(4,128)} %copy.131), calls=%async_computation.2 | async-start | bytes 786432 | tf_op jit(solution)/shard_map/all_to_all | solution.py:60
  145.9 68.7 %reduce-scatter.2.cloned.1.call-start = ((), (), s32[]{:S(2)}) async-start(), calls=%async_computation.5 | async-start | bytes 2785280 | tf_op jit(solution)/shard_map/reduce_scatter | solution.py:205
  166.7 4.1 %copy-start.15 = (f32[128,1,256]{2,0,1:T(8,128)S(1)}, f32[128,1,256]{2,0,1:T(8,128)}, u32[]{:S(2)}) copy-start(f32[128,1,256]{2,0,1:T(8,128)} %copy.132) | copy-start | bytes 393220
  167.9 4.2 %collective-permute-start.7 = (f32[2,3,256]{2,0,1:T(2,128)S(1)}, f32[2,3,256]{2,0,1:T(2,128)S(1)}, u32[]{:S(2)}, u32[]{:S(2)}) collective-permute-start(f32[2,3,256]{2,0,1:T(2,128)S(1)} %slice.165), channel_id=1, source_target_pairs={{4,0},{8,4},{12,8},{16,12},{20,16},{24,20},{28,24},{32,28},{36,32}... | collective-permute-start | bytes 18440 | tf_op jit(solution)/shard_map/ppermute | solution.py:14
  177.5 3.1 %copy-start.20 = (bf16[128]{0:T(256)(128)(2,1)S(1)}, bf16[128]{0:T(256)(128)(2,1)}, u32[]{:S(2)}) copy-start(bf16[128]{0:T(256)(128)(2,1)} %pad.17.clone) | copy-start | bytes 772
  182.3 33.6 %copy-start.21 = (f32[128]{0:T(128)S(1)}, f32[128]{0:T(128)}, u32[]{:S(2)}) copy-start(f32[128]{0:T(128)} %get-tuple-element.52) | copy-start | bytes 1540
  182.4 33.6 %copy-start.23 = (f32[128]{0:T(128)S(1)}, f32[128]{0:T(128)}, u32[]{:S(2)}) copy-start(f32[128]{0:T(128)} %copy-done.22) | copy-start | bytes 1540
  215.8 12.0 %copy-start.16 = (f32[1,128,64,4]{1,3,0,2:T(4,128)S(1)}, f32[1,128,64,4]{1,3,0,2:T(4,128)}, u32[]{:S(2)}) copy-start(f32[1,128,64,4]{1,3,0,2:T(4,128)} %get-tuple-element.35) | copy-start | bytes 393220
  217.9 9.5 %collective-permute-start.8 = (bf16[1,128,1024]{2,1,0:T(8,128)(2,1)S(1)}, bf16[1,128,1024]{2,1,0:T(8,128)(2,1)S(1)}, u32[]{:S(2)}, u32[]{:S(2)}) collective-permute-start(bf16[1,128,1024]{2,1,0:T(8,128)(2,1)S(1)} %bitcast.192), channel_id=1, source_target_pairs={{0,2},{1,3},{2,0},{3,1},{4,6},{5,7},{6,4},{7,5},{8,10},{9,11},{10,... | collective-permute-start | bytes 786440 | tf_op jit(solution)/shard_map/ppermute | solution.py:25
  227.5 12.8 %collective-permute-start.9 = (bf16[2,1,128,1024]{3,2,1,0:T(8,128)(2,1)S(1)}, bf16[2,1,128,1024]{3,2,1,0:T(8,128)(2,1)S(1)}, u32[]{:S(2)}, u32[]{:S(2)}) collective-permute-start(bf16[2,1,128,1024]{3,2,1,0:T(8,128)(2,1)S(1)} %maximum_select_fusion.5), channel_id=1, source_target_pairs={{0,1},{1,0},{2,3},{3,2},{4,5},{5,4},{6,7},{7,6},{8,9},{9,8},{10,11... | collective-permute-start | bytes 1572872 | tf_op jit(solution)/shard_map/ppermute | solution.py:25
  (7 other events, 5.3 us)
Sparse Core Ops, SparseCore 0:
  11.3 88.2 all-gather.1
  182.5 32.1 reduce-scatter.1
where the time goes:
time: 251 us; the launch traced here: 249 us
  waiting for transfers between devices  132 us (53%)
  starting transfers between devices  42.9 us (17%)
  local copies, waits for them, and re-layouts  22.1 us (9%)
  other arithmetic  18.8 us (7%)
  matrix products  18.6 us (7%)
  between operations  14.7 us (6%)
    ppermute x8, waiting for transfers between devices, doubled_gather(): arrived = lax.ppermute(gathered, axis, route)  52.5 us
    reduce_scatter x1, waiting for transfers between devices, per_device(): lax.psum_scatter(payload, 'ch', scatter_dimension=0).astype(jnp.float32)  32 us
    all_gather x1, waiting for transfers between devices, per_device(): lax.all_gather(in_weight.reshape(in_weight.shape[0], -1), 'seq', axis=0,...  25 us
    all_to_all x2, starting transfers between devices, to_columns(): lax.all_to_all(signals, 'seq', split_axis=1, concat_axis=2, tiled=True)  17.7 us
    ppermute x8, starting transfers between devices, doubled_gather(): arrived = lax.ppermute(gathered, axis, route)  13.5 us
    all_to_all x1, waiting for transfers between devices, to_rows(): lax.all_to_all(pieces, 'seq', split_axis=0, concat_axis=0, tiled=True)  13.4 us
    all_to_all x1, starting transfers between devices, to_rows(): lax.all_to_all(pieces, 'seq', split_axis=0, concat_axis=0, tiled=True)  6.64 us
    all_to_all x2, waiting for transfers between devices, to_columns(): lax.all_to_all(signals, 'seq', split_axis=1, concat_axis=2, tiled=True)  5.28 us
  transfers between devices with their start and end apart: 15, of which 13 were waited for; matrix products, arithmetic and copies ran while one was open for 11% of the time, Pallas kernels for 0%

commit v1 on v0

--- a/solution.py
+++ b/solution.py
@@ -6,6 +6,12 @@
 
 epsilon = 1e-05
 highest = lax.Precision.HIGHEST
+
+
+def gather_from_all(x, axis, dim):
+    devices = lax.axis_size(axis)
+    repeats = [devices if d == dim else 1 for d in range(x.ndim)]
+    return lax.all_to_all(jnp.tile(x, repeats), axis, split_axis=dim, concat_axis=dim, tiled=True)
 
 
 def passed_along(block, axis, distance):
@@ -130,7 +136,7 @@
     inv_rms = lax.rsqrt(jnp.mean(wide_inputs * wide_inputs, axis=1, keepdims=True) + epsilon)
     normed = (wide_inputs * inv_rms * norm_gain).astype(jnp.bfloat16)
     in_panel, out_panel = (
-        lax.all_gather(in_weight.reshape(in_weight.shape[0], -1), "seq", axis=0, tiled=True),
+        gather_from_all(in_weight.reshape(in_weight.shape[0], -1), "seq", 0),
         doubled_gather(out_weight.T, "seq").T,
     )
     in_flat = in_panel.reshape(model_width, 3 * slab_width)

time: 251 us -> 364 us (1.45)
  waiting for transfers between devices: 132 us -> 235 us
  starting transfers between devices: 42.9 us -> 51.6 us
    ppermute x8, waiting for transfers between devices: 52.5 us -> 181 us  [doubled_gather(): arrived = lax.ppermute(gathered, axis, route)]
    all_gather x1 -> x0, waiting for transfers between devices: 25 us -> none  [per_device(): lax.all_gather(in_weight.reshape(in_weight.shape[0], -1), 'seq', axis=0,...]
    all_to_all x0 -> x1, starting transfers between devices: none -> 12.3 us  [gather_from_all(): lax.all_to_all(jnp.tile(x, repeats), axis, split_axis=dim, concat_axis=di...]
    ppermute x8, starting transfers between devices: 13.5 us -> 8.18 us  [doubled_gather(): arrived = lax.ppermute(gathered, axis, route)]
    another operation x0 -> x2, local copies, waits for them, and re-layouts: none -> 4.34 us  [gather_from_all(): jnp.tile(x, repeats)]
  transfers between devices with their start and end apart: 15 -> 15, of which waited for: 13 -> 12; matrix products, arithmetic and copies ran while one was open for 11% -> 7% of each run, Pallas kernels for 0% -> 0%
where the time goes in v1:
time: 364 us; the launch traced here: 363 us
  waiting for transfers between devices  235 us (65%)
  starting transfers between devices  51.6 us (14%)
  local copies, waits for them, and re-layouts  24.5 us (7%)
  matrix products  19.6 us (5%)
  other arithmetic  16.9 us (5%)
  between operations  14.8 us (4%)
    ppermute x8, waiting for transfers between devices, doubled_gather(): arrived = lax.ppermute(gathered, axis, route)  181 us
    reduce_scatter x1, waiting for transfers between devices, per_device(): lax.psum_scatter(payload, 'ch', scatter_dimension=0).astype(jnp.float32)  31.8 us
    all_to_all x2, starting transfers between devices, to_columns(): lax.all_to_all(signals, 'seq', split_axis=1, concat_axis=2, tiled=True)  19.6 us
    all_to_all x1, waiting for transfers between devices, to_rows(): lax.all_to_all(pieces, 'seq', split_axis=0, concat_axis=0, tiled=True)  13.3 us
    all_to_all x1, starting transfers between devices, gather_from_all(): lax.all_to_all(jnp.tile(x, repeats), axis, split_axis=dim, concat_axis=di...  12.3 us
    ppermute x8, starting transfers between devices, doubled_gather(): arrived = lax.ppermute(gathered, axis, route)  8.18 us
  transfers between devices with their start and end apart: 15, of which 12 were waited for; matrix products, arithmetic and copies ran while one was open for 7% of the time, Pallas kernels for 0%

profile of v1, /device:TPU:2, one launch (start us, length us, event | category | flops | bytes accessed | tf_op | source)
XLA Modules:
  0.0 362.6 jit_solution(17371574400792910458)
XLA Ops:
  8.1 3.4 tile.9
  11.5 12.3 %all-to-all-start = ((bf16[64,64,768]{2,1,0:T(8,128)(2,1)}), bf16[64,64,768]{2,1,0:T(8,128)(2,1)}, u32[]{:S(2)}, u32[]{:S(2)}) async-start(bf16[64,64,768]{2,1,0:T(8,128)(2,1)} %tile.9), calls=%async_computation | async-start | bytes 12582912 | tf_op jit(solution)/shard_map/all_to_all | solution.py:14
  23.9 2.4 collective-permute-start.1
  26.9 14.4 %collective-permute-done.1 = bf16[64,256]{1,0:T(8,128)(2,1)S(1)} collective-permute-done((bf16[64,256]{1,0:T(8,128)(2,1)S(1)}, bf16[64,256]{1,0:T(8,128)(2,1)S(1)}, u32[]{:S(2)}, u32[]{:S(2)}) %collective-permute-start.1) | collective-permute-done | bytes 32800 | tf_op jit(solution)/shard_map/ppermute | solution.py:31
  41.9 4.3 %collective-permute-done.2 = bf16[2,64,256]{2,1,0:T(8,128)(2,1)S(1)} collective-permute-done((bf16[2,64,256]{2,1,0:T(8,128)(2,1)S(1)}, bf16[2,64,256]{2,1,0:T(8,128)(2,1)S(1)}, u32[]{:S(2)}, u32[]{:S(2)}) %collective-permute-start.2) | collective-permute-done | bytes 65568 | tf_op jit(solution)/shard_map/ppermute | solution.py:31
  46.2 2.6 collective-permute-start.3
  48.8 121.6 %collective-permute-done.3 = bf16[2,2,64,256]{3,2,0,1:T(8,128)(2,1)S(1)} collective-permute-done((bf16[2,2,64,256]{3,2,0,1:T(8,128)(2,1)S(1)}, bf16[2,2,64,256]{3,2,0,1:T(8,128)(2,1)S(1)}, u32[]{:S(2)}, u32[]{:S(2)}) %collective-permute-start.3) | collective-permute-done | bytes 131104 | tf_op jit(solution)/shard_map/ppermute | solution.py:31
  171.3 11.5 %collective-permute-done.4 = bf16[2,2,2,64,256]{4,3,0,1,2:T(8,128)(2,1)S(1)} collective-permute-done((bf16[2,2,2,64,256]{4,3,0,1,2:T(8,128)(2,1)S(1)}, bf16[2,2,2,64,256]{4,3,0,1,2:T(8,128)(2,1)S(1)}, u32[]{:S(2)}, u32[]{:S(2)}) %collective-permute-start.4) | collective-permute-done | bytes 262176 | tf_op jit(solution)/shard_map/ppermute | solution.py:31
  186.4 8.1 %collective-permute-done.5 = bf16[2,2,2,2,64,256]{5,4,0,1,2,3:T(8,128)(2,1)S(1)} collective-permute-done((bf16[2,2,2,2,64,256]{5,4,0,1,2,3:T(8,128)(2,1)S(1)}, bf16[2,2,2,2,64,256]{5,4,0,1,2,3:T(8,128)(2,1)S(1)}, u32[]{:S(2)}, u32[]{:S(2)}) %collective-permute-start.5) | collective-permute-done | bytes 524320 | tf_op jit(solution)/shard_map/ppermute | solution.py:31
  197.5 9.9 %all-to-all-start.2 = ((f32[1,256,128]{2,0,1:T(1,128)}), f32[1,256,128]{2,0,1:T(1,128)}, u32[]{:S(2)}, u32[]{:S(2)}) async-start(f32[1,256,128]{2,0,1:T(1,128)} %bitcast.1), calls=%async_computation.2 | async-start | bytes 262144 | tf_op jit(solution)/shard_map/all_to_all | solution.py:58
  207.5 3.9 %convolution_convert_fusion.1 = bf16[128,768]{1,0:T(8,128)(2,1)S(1)} fusion(bf16[4096,768]{1,0:T(8,128)(2,1)} %bitcast.6, bf16[128,4096]{1,0:T(8,128)(2,1)S(1)} %copy-done, f32[4096]{0:T(1024)S(1)} %copy-done.24, f32[128]{0:T(128)S(1)} %get-tuple-element.53), kind=kOutput, calls=%fused_computation.26 | convolution fusion | flops 807501824 | bytes 7553536 | tf_op jit(solution)/shard_map/dot_general | solution.py:143
  212.0 2.0 collective-permute-start
  215.5 3.7 %collective-permute-done = bf16[2,3,256]{2,0,1:T(2,128)(2,1)S(1)} collective-permute-done((bf16[2,3,256]{2,0,1:T(2,128)(2,1)}, bf16[2,3,256]{2,0,1:T(2,128)(2,1)S(1)}, u32[]{:S(2)}, u32[]{:S(2)}) %collective-permute-start) | collective-permute-done | bytes 3104 | tf_op jit(solution)/shard_map/ppermute | solution.py:20
  220.2 1.8 copy.120
  221.9 9.6 %all-to-all-start.1 = ((f32[2,256,128]{2,0,1:T(2,128)}), f32[2,256,128]{2,0,1:T(2,128)}, u32[]{:S(2)}, u32[]{:S(2)}) async-start(f32[2,256,128]{2,0,1:T(2,128)} %copy.120), calls=%async_computation.1 | async-start | bytes 524288 | tf_op jit(solution)/shard_map/all_to_all | solution.py:58
  235.4 2.3 convolution_bitcast_fusion.1
  237.7 5.3 %all-to-all-done.1 = f32[2,256,128]{2,0,1:T(2,128)} async-done(((f32[2,256,128]{2,0,1:T(2,128)}), f32[2,256,128]{2,0,1:T(2,128)}, u32[]{:S(2)}, u32[]{:S(2)}) %all-to-all-start.1) | async-done | bytes 262176 | tf_op jit(solution)/shard_map/all_to_all | solution.py:58
  243.0 1.6 convolution_bitcast_fusion
  250.2 6.6 %all-to-all-start.3 = ((f32[64,3,4,128]{3,2,1,0:T(4,128)}), f32[64,3,4,128]{3,2,1,0:T(4,128)}, u32[]{:S(2)}, u32[]{:S(2)}) async-start(f32[64,3,4,128]{3,2,1,0:T(4,128)} %copy.131), calls=%async_computation.3 | async-start | bytes 786432 | tf_op jit(solution)/shard_map/all_to_all | solution.py:66
  257.6 13.3 %all-to-all-done.3 = f32[64,3,4,128]{3,2,1,0:T(4,128)} async-done(((f32[64,3,4,128]{3,2,1,0:T(4,128)}), f32[64,3,4,128]{3,2,1,0:T(4,128)}, u32[]{:S(2)}, u32[]{:S(2)}) %all-to-all-start.3) | async-done | bytes 393248 | tf_op jit(solution)/shard_map/all_to_all | solution.py:66
  270.9 1.8 slice_multiply_fusion.6
  272.7 1.7 copy.135
  274.4 1.7 copy.134
  278.5 2.8 collective-permute-start.7
  281.3 1.7 copy.132
  283.0 1.8 convolution_convert_fusion
  286.0 5.0 %fusion.90 = (bf16[128,4096]{1,0:T(8,128)(2,1)S(1)}, f32[128]{0:T(128)S(1)}) fusion(bf16[128,4096]{1,0:T(8,128)(2,1)S(1)} %copy-done, f32[4096]{0:T(1024)S(1)} %copy-done.25, bf16[128,768]{0,1:T(8,128)(2,1)S(1)} %bitcast.207, bf16[4096,768]{1,0:T(8,128)(2,1)} %bitcast.6), kind=kOutput, calls=%fused_computation.176 | convolution fusion | flops 807927680 | bytes 8602112 | tf_op jit(solution)/shard_map/dot_general | solution.py:190
  294.2 1.6 pad_maximum_fusion
  296.1 31.8 %reduce-scatter.2.cloned.1.call-done = bf16[1,128,2176]{2,1,0:T(8,128)(2,1)} async-done(((bf16[4,128,2176]{2,1,0:T(8,128)(2,1)}), bf16[1,128,2176]{2,1,0:T(8,128)(2,1)}) %reduce-scatter.2.cloned.1.call-update) | async-done | bytes 557072 | tf_op jit(solution)/shard_map/reduce_scatter | solution.py:211
  329.2 1.9 fusion.29
  332.6 8.0 %collective-permute-done.8 = bf16[1,128,1024]{2,1,0:T(8,128)(2,1)S(1)} collective-permute-done((bf16[1,128,1024]{2,1,0:T(8,128)(2,1)S(1)}, bf16[1,128,1024]{2,1,0:T(8,128)(2,1)S(1)}, u32[]{:S(2)}, u32[]{:S(2)}) %collective-permute-start.8) | collective-permute-done | bytes 262176 | tf_op jit(solution)/shard_map/ppermute | solution.py:31
  341.8 11.7 %collective-permute-done.9 = bf16[2,1,128,1024]{3,2,1,0:T(8,128)(2,1)S(1)} collective-permute-done((bf16[2,1,128,1024]{3,2,1,0:T(8,128)(2,1)S(1)}, bf16[2,1,128,1024]{3,2,1,0:T(8,128)(2,1)S(1)}, u32[]{:S(2)}, u32[]{:S(2)}) %collective-permute-start.9) | collective-permute-done | bytes 524320 | tf_op jit(solution)/shard_map/ppermute | solution.py:31
  (153 shorter events, 35.7 us)
Async XLA Ops:
  11.5 12.3 %copy-start.22 = (bf16[256,64]{0,1:T(8,128)(2,1)S(1)}, bf16[256,64]{0,1:T(8,128)(2,1)}, u32[]{:S(2)}) copy-start(bf16[256,64]{0,1:T(8,128)(2,1)} %param.14) | copy-start | bytes 98308
  11.5 14.7 %copy-start.26 = (f32[3,3,256]{2,1,0:T(4,128)S(1)}, f32[3,3,256]{2,1,0:T(4,128)}, u32[]{:S(2)}) copy-start(f32[3,3,256]{2,1,0:T(4,128)} %param.11) | copy-start | bytes 27652
  11.5 186.0 %all-to-all-start = ((bf16[64,64,768]{2,1,0:T(8,128)(2,1)}), bf16[64,64,768]{2,1,0:T(8,128)(2,1)}, u32[]{:S(2)}, u32[]{:S(2)}) async-start(bf16[64,64,768]{2,1,0:T(8,128)(2,1)} %tile.9), calls=%async_computation | async-start | bytes 12582912 | tf_op jit(solution)/shard_map/all_to_all | solution.py:14
  23.9 17.4 %collective-permute-start.1 = (bf16[64,256]{1,0:T(8,128)(2,1)S(1)}, bf16[64,256]{1,0:T(8,128)(2,1)S(1)}, u32[]{:S(2)}, u32[]{:S(2)}) collective-permute-start(bf16[64,256]{1,0:T(8,128)(2,1)S(1)} %bitcast.214), channel_id=1, source_target_pairs={{0,128},{4,132},{8,136},{12,140},{16,144},{20,148},{24,152},{28,15... | collective-permute-start | bytes 98312 | tf_op jit(solution)/shard_map/ppermute | solution.py:31
  41.3 4.9 %collective-permute-start.2 = (bf16[2,64,256]{2,1,0:T(8,128)(2,1)S(1)}, bf16[2,64,256]{2,1,0:T(8,128)(2,1)S(1)}, u32[]{:S(2)}, u32[]{:S(2)}) collective-permute-start(bf16[2,64,256]{2,1,0:T(8,128)(2,1)S(1)} %maximum_select_fusion.8), channel_id=1, source_target_pairs={{0,64},{4,68},{8,72},{12,76},{16,80},{20,84},{24,88},{28,92},{32,9... | collective-permute-start | bytes 196616 | tf_op jit(solution)/shard_map/ppermute | solution.py:31
  46.2 124.2 %collective-permute-start.3 = (bf16[2,2,64,256]{3,2,0,1:T(8,128)(2,1)S(1)}, bf16[2,2,64,256]{3,2,0,1:T(8,128)(2,1)S(1)}, u32[]{:S(2)}, u32[]{:S(2)}) collective-permute-start(bf16[2,2,64,256]{3,2,0,1:T(8,128)(2,1)S(1)} %maximum_select_fusion.7), channel_id=1, source_target_pairs={{0,32},{4,36},{8,40},{12,44},{16,48},{20,52},{24,56},{28,60},{32,0... | collective-permute-start | bytes 393224 | tf_op jit(solution)/shard_map/ppermute | solution.py:31
  48.7 136.7 %copy-start.23 = (f32[128,256]{1,0:T(8,128)S(1)}, f32[128,256]{1,0:T(8,128)}, u32[]{:S(2)}) copy-start(f32[128,256]{1,0:T(8,128)} %param.12) | copy-start | bytes 393220
  170.4 12.3 %collective-permute-start.4 = (bf16[2,2,2,64,256]{4,3,0,1,2:T(8,128)(2,1)S(1)}, bf16[2,2,2,64,256]{4,3,0,1,2:T(8,128)(2,1)S(1)}, u32[]{:S(2)}, u32[]{:S(2)}) collective-permute-start(bf16[2,2,2,64,256]{4,3,0,1,2:T(8,128)(2,1)S(1)} %maximum_select_fusion.6), channel_id=1, source_target_pairs={{0,16},{4,20},{8,24},{12,28},{16,0},{20,4},{24,8},{28,12},{32,48},... | collective-permute-start | bytes 786440 | tf_op jit(solution)/shard_map/ppermute | solution.py:31
  182.8 11.6 %collective-permute-start.5 = (bf16[2,2,2,2,64,256]{5,4,0,1,2,3:T(8,128)(2,1)S(1)}, bf16[2,2,2,2,64,256]{5,4,0,1,2,3:T(8,128)(2,1)S(1)}, u32[]{:S(2)}, u32[]{:S(2)}) collective-permute-start(bf16[2,2,2,2,64,256]{5,4,0,1,2,3:T(8,128)(2,1)S(1)} %maximum_select_fusion.3), channel_id=1, source_target_pairs={{0,8},{4,12},{8,0},{12,4},{16,24},{20,28},{24,16},{28,20},{32,40},... | collective-permute-start | bytes 1572872 | tf_op jit(solution)/shard_map/ppermute | solution.py:31
  184.0 2.2 copy-start.15
  186.3 8.4 %copy-start = (bf16[128,4096]{1,0:T(8,128)(2,1)S(1)}, bf16[128,4096]{1,0:T(8,128)(2,1)}, u32[]{:S(2)}) copy-start(bf16[128,4096]{1,0:T(8,128)(2,1)} %param.8) | copy-start | bytes 3145732
  194.5 2.7 collective-permute-start.6
  195.5 12.0 %copy-start.30 = (f32[128]{0:T(128)}, f32[128]{0:T(128)S(1)}, u32[]{:S(2)}) copy-start(f32[128]{0:T(128)S(1)} %get-tuple-element.53) | copy-start | bytes 1540
  197.3 10.2 %copy-start.24 = (f32[4096]{0:T(1024)S(1)}, f32[4096]{0:T(1024)}, u32[]{:S(2)}) copy-start(f32[4096]{0:T(1024)} %param.9) | copy-start | bytes 49156
  197.5 24.4 %all-to-all-start.2 = ((f32[1,256,128]{2,0,1:T(1,128)}), f32[1,256,128]{2,0,1:T(1,128)}, u32[]{:S(2)}, u32[]{:S(2)}) async-start(f32[1,256,128]{2,0,1:T(1,128)} %bitcast.1), calls=%async_computation.2 | async-start | bytes 262144 | tf_op jit(solution)/shard_map/all_to_all | solution.py:58
  207.5 6.5 %copy-start.8 = (bf16[128,4096]{1,0:T(8,128)(2,1)S(1)}, bf16[128,4096]{1,0:T(8,128)(2,1)}, u32[]{:S(2)}) copy-start(bf16[128,4096]{1,0:T(8,128)(2,1)} %param.15) | copy-start | bytes 3145732
  212.0 7.2 %collective-permute-start = (bf16[2,3,256]{2,0,1:T(2,128)(2,1)}, bf16[2,3,256]{2,0,1:T(2,128)(2,1)S(1)}, u32[]{:S(2)}, u32[]{:S(2)}) collective-permute-start(bf16[2,3,256]{2,0,1:T(2,128)(2,1)} %bitcast.7), channel_id=1, source_target_pairs={{0,4},{4,8},{8,12},{12,16},{16,20},{20,24},{24,28},{28,32},{32,36}... | collective-permute-start | bytes 9224 | tf_op jit(solution)/shard_map/ppermute | solution.py:20
  215.5 3.9 %copy-start.9 = (f32[128,256]{1,0:T(8,128)S(1)}, f32[128,256]{1,0:T(8,128)}, u32[]{:S(2)}) copy-start(f32[128,256]{1,0:T(8,128)} %convolution_bitcast_fusion.3) | copy-start | bytes 393220
  221.9 21.1 %all-to-all-start.1 = ((f32[2,256,128]{2,0,1:T(2,128)}), f32[2,256,128]{2,0,1:T(2,128)}, u32[]{:S(2)}, u32[]{:S(2)}) async-start(f32[2,256,128]{2,0,1:T(2,128)} %copy.120), calls=%async_computation.1 | async-start | bytes 524288 | tf_op jit(solution)/shard_map/all_to_all | solution.py:58
  243.0 2.7 copy-start.10
  243.0 2.7 copy-start.11
  243.0 2.7 copy-start.12
  248.6 27.4 %copy-start.27 = (f32[256]{0:T(256)S(1)}, f32[256]{0:T(256)}, u32[]{:S(2)}) copy-start(f32[256]{0:T(256)} %param.13) | copy-start | bytes 3076
  250.2 20.7 %all-to-all-start.3 = ((f32[64,3,4,128]{3,2,1,0:T(4,128)}), f32[64,3,4,128]{3,2,1,0:T(4,128)}, u32[]{:S(2)}, u32[]{:S(2)}) async-start(f32[64,3,4,128]{3,2,1,0:T(4,128)} %copy.131), calls=%async_computation.3 | async-start | bytes 786432 | tf_op jit(solution)/shard_map/all_to_all | solution.py:66
  256.9 71.0 %reduce-scatter.2.cloned.1.call-start = ((), (), s32[]{:S(2)}) async-start(), calls=%async_computation.5 | async-start | bytes 2785280 | tf_op jit(solution)/shard_map/reduce_scatter | solution.py:211
  278.5 6.4 %collective-permute-start.7 = (f32[2,3,256]{2,0,1:T(2,128)}, f32[2,3,256]{2,0,1:T(2,128)}, u32[]{:S(2)}, u32[]{:S(2)}) collective-permute-start(f32[2,3,256]{2,0,1:T(2,128)} %slice.165), channel_id=1, source_target_pairs={{4,0},{8,4},{12,8},{16,12},{20,16},{24,20},{28,24},{32,28},{36,32}... | collective-permute-start | bytes 18440 | tf_op jit(solution)/shard_map/ppermute | solution.py:20
  291.3 2.8 copy-start.28
  295.8 33.4 %copy-start.29 = (f32[128]{0:T(128)S(1)}, f32[128]{0:T(128)}, u32[]{:S(2)}) copy-start(f32[128]{0:T(128)} %get-tuple-element.52) | copy-start | bytes 1540
  295.8 33.4 %copy-start.31 = (f32[128]{0:T(128)S(1)}, f32[128]{0:T(128)}, u32[]{:S(2)}) copy-start(f32[128]{0:T(128)} %copy-done.30) | copy-start | bytes 1540
  329.0 12.0 %copy-start.21 = (f32[1,128,64,4]{1,3,0,2:T(4,128)S(1)}, f32[1,128,64,4]{1,3,0,2:T(4,128)}, u32[]{:S(2)}) copy-start(f32[1,128,64,4]{1,3,0,2:T(4,128)} %get-tuple-element.35) | copy-start | bytes 393220
  331.1 9.5 %collective-permute-start.8 = (bf16[1,128,1024]{2,1,0:T(8,128)(2,1)S(1)}, bf16[1,128,1024]{2,1,0:T(8,128)(2,1)S(1)}, u32[]{:S(2)}, u32[]{:S(2)}) collective-permute-start(bf16[1,128,1024]{2,1,0:T(8,128)(2,1)S(1)} %bitcast.193), channel_id=1, source_target_pairs={{0,2},{1,3},{2,0},{3,1},{4,6},{5,7},{6,4},{7,5},{8,10},{9,11},{10,... | collective-permute-start | bytes 786440 | tf_op jit(solution)/shard_map/ppermute | solution.py:31
  340.7 12.8 %collective-permute-start.9 = (bf16[2,1,128,1024]{3,2,1,0:T(8,128)(2,1)S(1)}, bf16[2,1,128,1024]{3,2,1,0:T(8,128)(2,1)S(1)}, u32[]{:S(2)}, u32[]{:S(2)}) collective-permute-start(bf16[2,1,128,1024]{3,2,1,0:T(8,128)(2,1)S(1)} %maximum_select_fusion.5), channel_id=1, source_target_pairs={{0,1},{1,0},{2,3},{3,2},{4,5},{5,4},{6,7},{7,6},{8,9},{9,8},{10,11... | collective-permute-start | bytes 1572872 | tf_op jit(solution)/shard_map/ppermute | solution.py:31
  (15 other events, 17.5 us)
Sparse Core Ops, SparseCore 0:
  295.9 31.8 reduce-scatter.1
